TPU v7x, 256 devices: a whole 4x4x8 slice. The times are simulated.
256 devices in a mesh: stn: 64 (over y, z, core), sec: 4 (over x).
Axes of the slice: x: 4, y: 4, z: 8, core: 2. Of those that a mesh axis runs over, the one named last changes fastest.
Arguments:
- voltages: bfloat16 [2, 1024, 569344], P(None, ('stn', 'sec')), may hold values from -6 to 6
- fir_taps: float32 [12, 4096], replicated, may hold values from -1.75 to 1.75
- cor_channels: int32 [256], replicated, may hold values from 0 to 4095, as said below
- beam_channels: int32 [256], replicated, may hold values from 1 to 4094, as said below
- cor_gain: float32 [256], replicated, as said below
- beam_gain: float32 [256], replicated, as said below
- beam_stations: int32 [16, 512], replicated, may hold values from 0 to 511
- beam_codes: int32 [16, 512], replicated, may hold values from 0 to 255
Outputs:
- visibilities: bfloat16 [256, 2, 1024, 1024], P(('stn', 'sec'))
- beams: bfloat16 [256, 16, 2, 256], P(('stn', 'sec'))
Inputs may be any that keep to these rules, and one draw needn't show every extreme that they name: cor_channels and beam_channels together are 512 distinct transform channels. None of beam_channels appears in cor_channels. `cor_gain`: positive. `beam_gain`: positive.
All inputs are finite; a program needn't handle non-finite values.
Results may differ from a plain program's by a relative error of at most 0.0085.
Values may be sent and summed in bfloat16 or wider, within the bound.
No kernel may reach another device: no remote copies, remote signals or barrier semaphores. Data moves between devices by JAX's collectives and lax.ppermute only.
A program may use at most 128 MiB of HBM per device.

v0:
```python
import math
import jax
import jax.numpy as jnp
from jax import lax
from jax.sharding import PartitionSpec as P

STATIONS = 512
epsilon = 1e-05


def make_tables(channel_of, points):
    sample_index = jnp.arange(points, dtype=jnp.int32)
    phase_turns = channel_of[:, None] * sample_index[None, :] % points
    phase_angle = phase_turns.astype(jnp.float32) * (2.0 * math.pi / points)
    table_scale = 1.0 / math.sqrt(points)
    cos_table = (jnp.cos(phase_angle) * table_scale).astype(jnp.bfloat16)
    sin_table = (jnp.sin(phase_angle) * table_scale).astype(jnp.bfloat16)
    return (cos_table, sin_table)


def make_weights(beam_stations, beam_codes, stations):
    station_ids = jnp.arange(stations, dtype=jnp.int32)
    onehot = (beam_stations[:, :, None] == station_ids[None, None, :]).astype(jnp.float32)
    amplitude = (1 + beam_codes // 64).astype(jnp.float32)
    phase_angle = (beam_codes % 64).astype(jnp.float32) * (2.0 * math.pi / 64.0)
    weight_re = jnp.einsum("bk,bks->bs", amplitude * jnp.cos(phase_angle), onehot)
    weight_im = jnp.einsum("bk,bks->bs", amplitude * jnp.sin(phase_angle), onehot)
    return (weight_re.astype(jnp.bfloat16), weight_im.astype(jnp.bfloat16))


def polyphase(in_block, fir_taps, spectra):
    tap_count, points = fir_taps.shape
    framed = in_block.reshape(in_block.shape[0], in_block.shape[1], -1, points)
    summed = jnp.zeros((framed.shape[0], framed.shape[1], spectra, points), jnp.float32)
    for tap_index in range(tap_count):
        summed = summed + fir_taps[tap_index] * framed[
            :, :, tap_index : tap_index + spectra, :
        ].astype(jnp.float32)
    return summed.astype(jnp.bfloat16)


def contract(left_rows, right_rows):
    contract_dims = (((1,), (1,)), ((), ()))
    return lax.dot_general(left_rows, right_rows, contract_dims, preferred_element_type=jnp.float32)


def spectrum(filtered, cos_table, sin_table, slot_gain):
    inputs_here, spectra, points = (filtered.shape[1], filtered.shape[2], filtered.shape[3])
    real_rows = filtered[0].reshape(inputs_here * spectra, points)
    imag_rows = filtered[1].reshape(inputs_here * spectra, points)
    spec_re = contract(cos_table, real_rows) + contract(sin_table, imag_rows)
    spec_im = contract(cos_table, imag_rows) - contract(sin_table, real_rows)
    combined = jnp.concatenate(
        [spec_re.reshape(-1, inputs_here, spectra), spec_im.reshape(-1, inputs_here, spectra)],
        axis=2,
    )
    return (combined * slot_gain[:, None, None]).astype(jnp.bfloat16)


def form_beams(beam_data, weight_re, weight_im):
    spectra = beam_data.shape[2] // 2
    samples = beam_data.reshape(beam_data.shape[0], -1, 2, beam_data.shape[2])
    with_re = jnp.einsum("bs,jspt->jbpt", weight_re, samples, preferred_element_type=jnp.float32)
    with_im = jnp.einsum("bs,jspt->jbpt", weight_im, samples, preferred_element_type=jnp.float32)
    out_re = with_re[..., :spectra] - with_im[..., spectra:]
    out_im = with_re[..., spectra:] + with_im[..., :spectra]
    return jnp.concatenate([out_re, out_im], axis=3)


def per_device(
    voltages, fir_taps, cor_channels, beam_channels, cor_gain, beam_gain, beam_stations, beam_codes
):
    tap_count, points = fir_taps.shape
    stn_count = lax.axis_size("stn")
    sec_count = lax.axis_size("sec")
    device_count = stn_count * sec_count
    inputs_here = voltages.shape[1]
    spectra = voltages.shape[2] // points - tap_count + 1
    filtered = polyphase(voltages, fir_taps, spectra)
    channel_of = jnp.concatenate([cor_channels, beam_channels])
    slot_gain = jnp.concatenate([cor_gain, beam_gain])
    cos_table, sin_table = make_tables(channel_of, points)
    weight_re, weight_im = make_weights(beam_stations, beam_codes, STATIONS)
    spectra_all = spectrum(filtered, cos_table, sin_table, slot_gain)
    outgoing = spectra_all.reshape(2, stn_count, sec_count, 1, 1, inputs_here, 2 * spectra)
    turned = lax.all_to_all(
        lax.all_to_all(outgoing, "stn", split_axis=1, concat_axis=3, tiled=True),
        "sec",
        split_axis=2,
        concat_axis=4,
        tiled=True,
    )
    received = turned.reshape(2, device_count * inputs_here, 2 * spectra)
    cor_data = received[0]
    beam_data = received[1:2]
    swapped = jnp.concatenate([cor_data[:, spectra:], -cor_data[:, :spectra]], axis=1)
    vis_re = contract(cor_data, cor_data) / spectra
    vis_im = contract(swapped, cor_data) / spectra
    visibilities = jnp.stack([vis_re, vis_im])[None].astype(jnp.bfloat16)
    raw_beams = form_beams(beam_data, weight_re, weight_im)
    local_power = jnp.sum(raw_beams * raw_beams, axis=(0, 2, 3))
    summed_power = lax.psum(local_power, ("stn", "sec"))
    beam_power = summed_power / (device_count * raw_beams.shape[2] * raw_beams.shape[3])
    beams = (raw_beams * lax.rsqrt(beam_power + epsilon)[None, :, None, None]).astype(jnp.bfloat16)
    return (visibilities, beams)


def solution(mesh):
    in_specs = (P(None, ("stn", "sec"), None), P(), P(), P(), P(), P(), P(), P())
    out_specs = (P(("stn", "sec"), None, None, None), P(("stn", "sec"), None, None, None))
    return jax.shard_map(
        per_device, mesh=mesh, in_specs=in_specs, out_specs=out_specs, check_vma=False
    )
```

profile of v0, /device:TPU:1, one launch (start us, length us, event | category | flops | bytes accessed | tf_op | source)
XLA Modules:
  0.0 348.5 jit_solution(4968068274849040461)
XLA Ops:
  0.6 1.8 fusion.60
  2.5 14.5 %reshape.175 = bf16[2,4,139,4096]{3,2,1,0:T(8,128)(2,1)} reshape(bf16[2,4,569344]{2,1,0:T(4,128)(2,1)} %param.8) | data formatting | bytes 18219008 | tf_op jit(solution)/shard_map/reshape | solution.py:33
  17.0 52.5 %add_convert_fusion = bf16[2,4,128,4096]{3,2,1,0:T(8,128)(2,1)} fusion(bf16[2,4,139,4096]{3,2,1,0:T(8,128)(2,1)} %reshape.175, f32[4096]{0:T(1024)S(1)} %bitcast.81, f32[4096]{0:T(1024)S(1)} %bitcast.82, f32[4096]{0:T(1024)S(1)} %bitcast.72, f32[4096]{0:T(1024)S(1)} %bitcast.73, f32[4096]{0:T(1024)S(1)} %bitcast.74, f32[4096]{0:T(1024)S(1)} %bitcast.75, ...), kind=kLoop, calls=%fused_computation.3 | loop fusion | flops 150994944 | bytes 109248512 | tf_op jit(solution)/shard_map/convert_element_type | solution.py:39
  69.5 4.0 %fusion.57 = (bf16[1,4,128,4096]{3,2,1,0:T(8,128)(2,1)S(1)}, bf16[1,4,128,4096]{3,2,1,0:T(8,128)(2,1)S(1)}) fusion(bf16[2,4,128,4096]{3,2,1,0:T(8,128)(2,1)} %add_convert_fusion), kind=kLoop, calls=%fused_computation.88 | loop fusion | bytes 16777216 | tf_op jit(solution)/shard_map/slice | solution.py:49
  73.6 31.8 %fusion.11 = f32[512,512]{1,0:T(8,128)S(1)} fusion(bf16[512,4096]{1,0:T(8,128)(2,1)S(1)} %bitcast.67, s32[512]{0:T(512)S(1)} %pad_add_fusion), kind=kOutput, calls=%fused_computation.21 | convolution fusion | flops 2181038080 | bytes 5244928 | tf_op jit(solution)/shard_map/dot_general | solution.py:44
  105.4 32.4 %fusion.10 = f32[512,512]{1,0:T(8,128)} fusion(bf16[512,4096]{1,0:T(8,128)(2,1)S(1)} %bitcast.69, s32[512]{0:T(512)S(1)} %pad_add_fusion), kind=kOutput, calls=%fused_computation.20 | convolution fusion | flops 2181038080 | bytes 5244928 | tf_op jit(solution)/shard_map/dot_general | solution.py:44
  137.7 32.1 %fusion.17 = f32[512,512]{1,0:T(8,128)S(1)} fusion(f32[512,512]{1,0:T(8,128)S(1)} %fusion.11, bf16[512,4096]{1,0:T(8,128)(2,1)S(1)} %bitcast.70, s32[512]{0:T(512)S(1)} %pad_add_fusion), kind=kOutput, calls=%fused_computation.29 | convolution fusion | flops 2181300224 | bytes 6293504 | tf_op jit(solution)/shard_map/dot_general | solution.py:44
  169.8 0.4 concatenate.56
  170.2 34.4 %fusion.18 = f32[512,512]{1,0:T(8,128)S(1)} fusion(f32[512,512]{1,0:T(8,128)} %fusion.10, bf16[512,4096]{1,0:T(8,128)(2,1)} %bitcast.68, s32[512]{0:T(512)S(1)} %pad_add_fusion), kind=kOutput, calls=%fused_computation.30 | convolution fusion | flops 2181300224 | bytes 6293504 | tf_op jit(solution)/shard_map/dot_general | solution.py:44
  204.7 0.4 concatenate.57
  205.1 0.1 concatenate.59
  205.4 0.7 fusion.14
  206.1 41.5 %all_to_all.33 = bf16[2,64,4,1,1,4,256]{6,5,2,0,4,3,1:T(4,128)(2,1)S(1)} all-to-all(bf16[2,64,4,1,1,4,256]{6,5,2,0,4,3,1:T(4,128)(2,1)S(1)} %fusion.14), channel_id=1, replica_groups=mesh['stn'=64,'sec'=4] {'stn'}, dimensions={1} | all-to-all | bytes 2097152 | tf_op jit(solution)/shard_map/all_to_all | solution.py:87
  247.6 1.4 copy.38
  249.0 4.0 %all-to-all-start.1 = ((bf16[2,1,4,64,1,4,256]{6,5,3,0,4,1,2:T(4,128)(2,1)}), bf16[2,1,4,64,1,4,256]{6,5,3,0,4,1,2:T(4,128)(2,1)S(1)}, u32[]{:S(2)}, u32[]{:S(2)}) async-start(bf16[2,1,4,64,1,4,256]{6,5,3,0,4,1,2:T(4,128)(2,1)} %copy.38), calls=%async_computation.1 | async-start | bytes 2097152 | tf_op jit(solution)/shard_map/all_to_all | solution.py:86
  253.0 0.2 multiply_bitcast_fusion.1
  253.2 3.2 fusion
  256.4 3.2 fusion.1
  259.6 8.3 %all-to-all-done.1 = bf16[2,1,4,64,1,4,256]{6,5,3,0,4,1,2:T(4,128)(2,1)S(1)} async-done(((bf16[2,1,4,64,1,4,256]{6,5,3,0,4,1,2:T(4,128)(2,1)}), bf16[2,1,4,64,1,4,256]{6,5,3,0,4,1,2:T(4,128)(2,1)S(1)}, u32[]{:S(2)}, u32[]{:S(2)}) %all-to-all-start.1) | async-done | bytes 1048608 | tf_op jit(solution)/shard_map/all_to_all | solution.py:86
  267.9 0.4 fusion.58
  268.3 0.2 copy.40
  268.5 0.3 reshape.176
  268.7 0.2 convolution_bitcast_fusion
  268.9 0.2 convolution_bitcast_fusion.1
  269.1 0.2 copy.39
  269.3 0.1 squeeze.3
  269.5 0.1 multiply_reduce_fusion
  269.6 0.7 fusion.15
  270.4 74.1 %psum.7 = f32[16]{0:T(128)S(1)} all-reduce(f32[16]{0:T(128)S(1)} %multiply_reduce_fusion), channel_id=1, replica_groups=mesh['stn'=64,'sec'=4] {'stn','sec'}, use_global_device_ids=true, to_apply=%region_1.2 | all-reduce | flops 16 | bytes 128 | tf_op jit(solution)/shard_map/psum | solution.py:102
  344.5 0.6 copy.43
  345.1 0.7 fusion.16
  345.9 2.4 pad_maximum_fusion
  (22 shorter events, 0.4 us)
Async XLA Ops:
  69.5 4.0 %copy-start.4 = (s32[256]{0:T(256)S(1)}, s32[256]{0:T(256)}, u32[]{:S(2)}) copy-start(s32[256]{0:T(256)} %param.11) | copy-start | bytes 3076
  69.5 4.0 %copy-start.5 = (s32[256]{0:T(256)S(1)}, s32[256]{0:T(256)}, u32[]{:S(2)}) copy-start(s32[256]{0:T(256)} %param.10) | copy-start | bytes 3076
  73.5 31.8 %copy-start = (bf16[1,4,128,4096]{3,2,1,0:T(8,128)(2,1)}, bf16[1,4,128,4096]{3,2,1,0:T(8,128)(2,1)S(1)}, u32[]{:S(2)}) copy-start(bf16[1,4,128,4096]{3,2,1,0:T(8,128)(2,1)S(1)} %get-tuple-element.12) | copy-start | bytes 12582916
  170.2 34.8 %copy-start.2 = (f32[256]{0:T(256)S(1)}, f32[256]{0:T(256)}, u32[]{:S(2)}) copy-start(f32[256]{0:T(256)} %param.12) | copy-start | bytes 3076
  170.2 35.0 %copy-start.3 = (f32[256]{0:T(256)S(1)}, f32[256]{0:T(256)}, u32[]{:S(2)}) copy-start(f32[256]{0:T(256)} %param.13) | copy-start | bytes 3076
  204.7 48.4 %copy-start.1 = (s32[16,512]{1,0:T(8,128)S(1)}, s32[16,512]{1,0:T(8,128)}, u32[]{:S(2)}) copy-start(s32[16,512]{1,0:T(8,128)} %param.15) | copy-start | bytes 98308
  204.7 48.5 %copy-start.6 = (s32[16,512]{1,0:T(8,128)S(1)}, s32[16,512]{1,0:T(8,128)}, u32[]{:S(2)}) copy-start(s32[16,512]{1,0:T(8,128)} %param.14) | copy-start | bytes 98308
  249.0 18.9 %all-to-all-start.1 = ((bf16[2,1,4,64,1,4,256]{6,5,3,0,4,1,2:T(4,128)(2,1)}), bf16[2,1,4,64,1,4,256]{6,5,3,0,4,1,2:T(4,128)(2,1)S(1)}, u32[]{:S(2)}, u32[]{:S(2)}) async-start(bf16[2,1,4,64,1,4,256]{6,5,3,0,4,1,2:T(4,128)(2,1)} %copy.38), calls=%async_computation.1 | async-start | bytes 2097152 | tf_op jit(solution)/shard_map/all_to_all | solution.py:86
where the time goes:
time: 352 us; the launch traced here: 348 us
  matrix products  139 us (39%)
  blocking collectives  116 us (33%)
  other arithmetic  56.1 us (16%)
  local copies, waits for them, and re-layouts  24.4 us (7%)
  waiting for transfers between devices  8.26 us (2%)
  starting transfers between devices  4.03 us (1%)
    dot_general x6, matrix products, contract(): lax.dot_general(left_rows, right_rows, contract_dims, preferred_element_t...  132 us
    psum x1, blocking collectives, per_device(): summed_power = lax.psum(local_power, ('stn', 'sec'))  74.1 us
    convert_element_type x1, other arithmetic, polyphase(): return summed.astype(jnp.bfloat16)  52.5 us
    all_to_all x1, blocking collectives, per_device(): lax.all_to_all(outgoing, 'stn', split_axis=1, concat_axis=3, tiled=True)  41.5 us
    reshape x1, local copies, waits for them, and re-layouts, polyphase(): framed = in_block.reshape(in_block.shape[0], in_block.shape[1], -1, points)  14.5 us
    all_to_all x1, waiting for transfers between devices, per_device(): lax.all_to_all(lax.all_to_all(outgoing, 'stn', split_axis=1, concat_axis=...  8.26 us
  transfers between devices with their start and end apart: 1, of which 1 were waited for; matrix products, arithmetic and copies ran while one was open for 2% of the time, Pallas kernels for 0%

commit v1 on v0

--- a/solution.py
+++ b/solution.py
@@ -3,6 +3,7 @@
 import jax.numpy as jnp
 from jax import lax
 from jax.sharding import PartitionSpec as P
+from jax.lax import all_gather
 
 STATIONS = 512
 epsilon = 1e-05
@@ -99,7 +100,8 @@
     visibilities = jnp.stack([vis_re, vis_im])[None].astype(jnp.bfloat16)
     raw_beams = form_beams(beam_data, weight_re, weight_im)
     local_power = jnp.sum(raw_beams * raw_beams, axis=(0, 2, 3))
-    summed_power = lax.psum(local_power, ("stn", "sec"))
+    a_now = all_gather(local_power, axis_name=("stn", "sec"))
+    summed_power = jnp.sum(a_now, 0)
     beam_power = summed_power / (device_count * raw_beams.shape[2] * raw_beams.shape[3])
     beams = (raw_beams * lax.rsqrt(beam_power + epsilon)[None, :, None, None]).astype(jnp.bfloat16)
     return (visibilities, beams)

time: 352 us -> 356 us (1.011)
    unnamed x0 -> x1, blocking collectives: none -> 74.1 us
    psum x1 -> x0, blocking collectives: 74.1 us -> none  [per_device(): summed_power = lax.psum(local_power, ('stn', 'sec'))]
where the time goes in v1:
time: 356 us; the launch traced here: 353 us
  matrix products  140 us (39%)
  blocking collectives  116 us (33%)
  other arithmetic  56.8 us (16%)
  local copies, waits for them, and re-layouts  27.1 us (8%)
  waiting for transfers between devices  8.26 us (2%)
  starting transfers between devices  4.03 us (1%)
    dot_general x6, matrix products, contract(): lax.dot_general(left_rows, right_rows, contract_dims, preferred_element_t...  133 us
    unnamed x1, blocking collectives  74.1 us
    convert_element_type x1, other arithmetic, polyphase(): return summed.astype(jnp.bfloat16)  52.4 us
    all_to_all x1, blocking collectives, per_device(): lax.all_to_all(outgoing, 'stn', split_axis=1, concat_axis=3, tiled=True)  41.5 us
    reshape x1, local copies, waits for them, and re-layouts, polyphase(): framed = in_block.reshape(in_block.shape[0], in_block.shape[1], -1, points)  14.5 us
    all_to_all x1, waiting for transfers between devices, per_device(): lax.all_to_all(lax.all_to_all(outgoing, 'stn', split_axis=1, concat_axis=...  8.26 us
  transfers between devices with their start and end apart: 1, of which 1 were waited for; matrix products, arithmetic and copies ran while one was open for 2% of the time, Pallas kernels for 0%

profile of v1, /device:TPU:1, one launch (start us, length us, event | category | flops | bytes accessed | tf_op | source)
XLA Modules:
  0.0 352.8 jit_solution(5833188282569066548)
XLA Ops:
  0.6 1.8 fusion.60
  2.5 14.5 %reshape.179 = bf16[2,4,139,4096]{3,2,1,0:T(8,128)(2,1)} reshape(bf16[2,4,569344]{2,1,0:T(4,128)(2,1)} %param.8) | data formatting | bytes 18219008 | tf_op jit(solution)/shard_map/reshape | solution.py:34
  17.0 52.4 %add_convert_fusion = bf16[2,4,128,4096]{3,2,1,0:T(8,128)(2,1)} fusion(bf16[2,4,139,4096]{3,2,1,0:T(8,128)(2,1)} %reshape.179, f32[4096]{0:T(1024)S(1)} %bitcast.81, f32[4096]{0:T(1024)S(1)} %bitcast.82, f32[4096]{0:T(1024)S(1)} %bitcast.72, f32[4096]{0:T(1024)S(1)} %bitcast.73, f32[4096]{0:T(1024)S(1)} %bitcast.74, f32[4096]{0:T(1024)S(1)} %bitcast.75, ...), kind=kLoop, calls=%fused_computation.3 | loop fusion | flops 150994944 | bytes 109248512 | tf_op jit(solution)/shard_map/convert_element_type | solution.py:40
  69.4 4.0 %fusion.57 = (bf16[1,4,128,4096]{3,2,1,0:T(8,128)(2,1)S(1)}, bf16[1,4,128,4096]{3,2,1,0:T(8,128)(2,1)S(1)}) fusion(bf16[2,4,128,4096]{3,2,1,0:T(8,128)(2,1)} %add_convert_fusion), kind=kLoop, calls=%fused_computation.88 | loop fusion | bytes 16777216 | tf_op jit(solution)/shard_map/slice | solution.py:50
  73.4 31.8 %fusion.11 = f32[512,512]{1,0:T(8,128)S(1)} fusion(bf16[512,4096]{1,0:T(8,128)(2,1)S(1)} %bitcast.67, s32[512]{0:T(512)S(1)} %pad_add_fusion), kind=kOutput, calls=%fused_computation.21 | convolution fusion | flops 2181038080 | bytes 5244928 | tf_op jit(solution)/shard_map/dot_general | solution.py:45
  105.3 32.4 %fusion.10 = f32[512,512]{1,0:T(8,128)} fusion(bf16[512,4096]{1,0:T(8,128)(2,1)S(1)} %bitcast.69, s32[512]{0:T(512)S(1)} %pad_add_fusion), kind=kOutput, calls=%fused_computation.20 | convolution fusion | flops 2181038080 | bytes 5244928 | tf_op jit(solution)/shard_map/dot_general | solution.py:45
  137.6 32.1 %fusion.17 = f32[512,512]{1,0:T(8,128)S(1)} fusion(f32[512,512]{1,0:T(8,128)S(1)} %fusion.11, bf16[512,4096]{1,0:T(8,128)(2,1)S(1)} %bitcast.70, s32[512]{0:T(512)S(1)} %pad_add_fusion), kind=kOutput, calls=%fused_computation.29 | convolution fusion | flops 2181300224 | bytes 6293504 | tf_op jit(solution)/shard_map/dot_general | solution.py:45
  169.7 0.4 concatenate.56
  170.1 34.4 %fusion.18 = f32[512,512]{1,0:T(8,128)S(1)} fusion(f32[512,512]{1,0:T(8,128)} %fusion.10, bf16[512,4096]{1,0:T(8,128)(2,1)} %bitcast.68, s32[512]{0:T(512)S(1)} %pad_add_fusion), kind=kOutput, calls=%fused_computation.30 | convolution fusion | flops 2181300224 | bytes 6293504 | tf_op jit(solution)/shard_map/dot_general | solution.py:45
  204.6 0.4 concatenate.57
  205.3 0.7 fusion.14
  206.0 41.5 %all_to_all.33 = bf16[2,64,4,1,1,4,256]{6,5,2,0,4,3,1:T(4,128)(2,1)S(1)} all-to-all(bf16[2,64,4,1,1,4,256]{6,5,2,0,4,3,1:T(4,128)(2,1)S(1)} %fusion.14), channel_id=1, replica_groups=mesh['stn'=64,'sec'=4] {'stn'}, dimensions={1} | all-to-all | bytes 2097152 | tf_op jit(solution)/shard_map/all_to_all | solution.py:88
  247.5 1.4 copy.38
  248.9 4.0 %all-to-all-start.1 = ((bf16[2,1,4,64,1,4,256]{6,5,3,0,4,1,2:T(4,128)(2,1)}), bf16[2,1,4,64,1,4,256]{6,5,3,0,4,1,2:T(4,128)(2,1)S(1)}, u32[]{:S(2)}, u32[]{:S(2)}) async-start(bf16[2,1,4,64,1,4,256]{6,5,3,0,4,1,2:T(4,128)(2,1)} %copy.38), calls=%async_computation.1 | async-start | bytes 2097152 | tf_op jit(solution)/shard_map/all_to_all | solution.py:87
  252.9 0.2 multiply_bitcast_fusion.1
  253.1 3.2 fusion
  256.3 3.2 fusion.1
  259.5 8.3 %all-to-all-done.1 = bf16[2,1,4,64,1,4,256]{6,5,3,0,4,1,2:T(4,128)(2,1)S(1)} async-done(((bf16[2,1,4,64,1,4,256]{6,5,3,0,4,1,2:T(4,128)(2,1)}), bf16[2,1,4,64,1,4,256]{6,5,3,0,4,1,2:T(4,128)(2,1)S(1)}, u32[]{:S(2)}, u32[]{:S(2)}) %all-to-all-start.1) | async-done | bytes 1048608 | tf_op jit(solution)/shard_map/all_to_all | solution.py:87
  267.8 0.4 fusion.58
  268.2 0.2 copy.39
  268.4 0.1 squeeze.3
  268.5 0.8 fusion.59
  269.3 0.7 fusion.15
  270.0 1.0 copy.40
  271.0 1.8 reshape.180
  272.8 0.2 convolution_bitcast_fusion
  273.0 0.2 convolution_bitcast_fusion.1
  273.3 0.3 dynamic-update-slice
  273.6 74.1 %all-reduce = f32[4096]{0:T(1024)S(1)} all-reduce(f32[4096]{0:T(1024)S(1)} %dynamic-update-slice), channel_id=2, replica_groups=mesh['stn'=64,'sec'=4] {'stn','sec'}, use_global_device_ids=true, to_apply=%add | all-reduce | flops 4096 | bytes 32768
  347.9 0.6 copy.43
  348.5 1.7 fusion.16
  350.2 2.4 pad_maximum_fusion
  (26 shorter events, 0.7 us)
Async XLA Ops:
  69.4 4.0 %copy-start.4 = (s32[256]{0:T(256)S(1)}, s32[256]{0:T(256)}, u32[]{:S(2)}) copy-start(s32[256]{0:T(256)} %param.11) | copy-start | bytes 3076
  69.4 4.0 %copy-start.5 = (s32[256]{0:T(256)S(1)}, s32[256]{0:T(256)}, u32[]{:S(2)}) copy-start(s32[256]{0:T(256)} %param.10) | copy-start | bytes 3076
  73.4 31.8 %copy-start = (bf16[1,4,128,4096]{3,2,1,0:T(8,128)(2,1)}, bf16[1,4,128,4096]{3,2,1,0:T(8,128)(2,1)S(1)}, u32[]{:S(2)}) copy-start(bf16[1,4,128,4096]{3,2,1,0:T(8,128)(2,1)S(1)} %get-tuple-element.12) | copy-start | bytes 12582916
  170.1 34.8 %copy-start.2 = (f32[256]{0:T(256)S(1)}, f32[256]{0:T(256)}, u32[]{:S(2)}) copy-start(f32[256]{0:T(256)} %param.12) | copy-start | bytes 3076
  170.1 35.0 %copy-start.3 = (f32[256]{0:T(256)S(1)}, f32[256]{0:T(256)}, u32[]{:S(2)}) copy-start(f32[256]{0:T(256)} %param.13) | copy-start | bytes 3076
  204.5 48.4 %copy-start.1 = (s32[16,512]{1,0:T(8,128)S(1)}, s32[16,512]{1,0:T(8,128)}, u32[]{:S(2)}) copy-start(s32[16,512]{1,0:T(8,128)} %param.15) | copy-start | bytes 98308
  204.6 48.5 %copy-start.6 = (s32[16,512]{1,0:T(8,128)S(1)}, s32[16,512]{1,0:T(8,128)}, u32[]{:S(2)}) copy-start(s32[16,512]{1,0:T(8,128)} %param.14) | copy-start | bytes 98308
  248.9 18.9 %all-to-all-start.1 = ((bf16[2,1,4,64,1,4,256]{6,5,3,0,4,1,2:T(4,128)(2,1)}), bf16[2,1,4,64,1,4,256]{6,5,3,0,4,1,2:T(4,128)(2,1)S(1)}, u32[]{:S(2)}, u32[]{:S(2)}) async-start(bf16[2,1,4,64,1,4,256]{6,5,3,0,4,1,2:T(4,128)(2,1)} %copy.38), calls=%async_computation.1 | async-start | bytes 2097152 | tf_op jit(solution)/shard_map/all_to_all | solution.py:87
